TPU v7x, 512 devices: a whole 4x4x16 slice. The times are simulated.
512 devices in a mesh: req: 64 (over z, x), head: 8 (over y, core).
Axes of the slice: x: 4, y: 4, z: 16, core: 2. Of those that a mesh axis runs over, the one named last changes fastest.
Arguments:
- tokens: bfloat16 [128, 1024], P('req'), may hold values from -6 to 6
- self_keys: bfloat16 [128, 512, 1024], P('req', None, 'head'), may hold values from -240 to 240
- self_values: bfloat16 [128, 512, 1024], P('req', None, 'head'), may hold values from -6 to 6
- self_len: int32 [128], P('req'), may hold values from 1 to 512, as said below
- cross_keys: bfloat16 [128, 512, 1024], P('req', None, 'head'), may hold values from -240 to 240
- cross_values: bfloat16 [128, 512, 1024], P('req', None, 'head'), may hold values from -6 to 6
- cross_len: int32 [128], P('req'), may hold values from 1 to 512, as said below
- give_slot: int32 [64], P('req'), may hold values from 0 to 1
- w_query: bfloat16 [1024, 1024], P(None, 'head'), may hold values from -0.1875 to 0.1875
- w_key: bfloat16 [1024, 1024], P(None, 'head'), may hold values from -0.1875 to 0.1875
- w_value: bfloat16 [1024, 1024], P(None, 'head'), may hold values from -0.1875 to 0.1875
- w_out: bfloat16 [1024, 1024], P('head'), may hold values from -0.1875 to 0.1875
- w_cross_query: bfloat16 [1024, 1024], P(None, 'head'), may hold values from -0.1875 to 0.1875
- w_cross_out: bfloat16 [1024, 1024], P('head'), may hold values from -0.1875 to 0.1875
- w_up: bfloat16 [1024, 4096], P(None, 'head'), may hold values from -0.1875 to 0.1875
- w_down: bfloat16 [4096, 1024], P('head'), may hold values from -0.09375 to 0.09375
- gain_self: float32 [1024], replicated, may hold values from 0.1 to 1.9
- gain_cross: float32 [1024], replicated, may hold values from 0.1 to 1.9
- gain_final: float32 [1024], replicated, may hold values from 0.1 to 1.9
Outputs:
- decoded: bfloat16 [128, 1024], P('req')
- new_keys: bfloat16 [128, 1024], P('req', 'head')
- new_values: bfloat16 [128, 1024], P('req', 'head')
- moved_keys: bfloat16 [64, 512, 1024], P('req', None, 'head')
- moved_values: bfloat16 [64, 512, 1024], P('req', None, 'head')
Inputs may be any that keep to these rules, and one draw needn't show every extreme that they name: `self_len`: each request fills at least one slot; some request fills all 512. `cross_len`: each request has at least one encoder position; some request has 512.
All inputs are finite; a program needn't handle non-finite values.
Results may differ from a plain program's by a relative error of at most 0.039.
Values may be sent and summed in bfloat16 or wider, within the bound.
No kernel may reach another device: no remote copies, remote signals or barrier semaphores. Data moves between devices by JAX's collectives and lax.ppermute only.
A program may use at most 64 MiB of HBM per device.

v0:
```python
import jax
import jax.numpy as jnp
from jax import lax
from jax.sharding import PartitionSpec as P

HEAD_DIM = 64


def passed_along(block, axis, distance):
    devices = range(lax.axis_size(axis))
    route = [((i - distance) % len(devices), i) for i in devices]
    return lax.ppermute(block, axis, route)


def layer_norm(value, gain):
    mean = jnp.mean(value, axis=-1, keepdims=True)
    centred = value - mean
    spread = jnp.mean(centred * centred, axis=-1, keepdims=True)
    return centred * lax.rsqrt(spread + 1e-05) * gain


def attend(query, keys, values, lengths, fresh_key, fresh_value):
    count, span, width = keys.shape
    heads = width // HEAD_DIM
    block = min(512, span)
    query_heads = query.reshape(count, heads, HEAD_DIM)
    steps = (jnp.max(lengths) + block - 1) // block
    places = lax.iota(jnp.int32, block)

    def score_block(index, board):
        start = index * block
        piece = keys.reshape(count, block, heads, HEAD_DIM)
        scores = jnp.einsum("qhd,qshd->qhs", query_heads, piece, preferred_element_type=jnp.float32)
        valid = (start + places)[None, None, :] < lengths[:, None, None]
        scores = jnp.where(valid, scores, -jnp.inf)
        return scores

    board = lax.fori_loop(
        0, steps, score_block, jnp.full((count, heads, span), -jnp.inf, jnp.float32)
    )
    top = jnp.max(board, axis=2)
    if fresh_key is not None:
        own = jnp.sum(
            query_heads.astype(jnp.float32)
            * fresh_key.reshape(count, heads, HEAD_DIM).astype(jnp.float32),
            axis=2,
        )
        top = jnp.maximum(top, own)
    weights_all = jnp.exp(board - top[:, :, None])
    total = jnp.sum(weights_all, axis=2)

    def mix_block(index, accum):
        start = index * block
        weights = weights_all.astype(jnp.bfloat16)
        piece = values.reshape(count, block, heads, HEAD_DIM)
        return accum + jnp.einsum(
            "qhs,qshd->qhd", weights, piece, preferred_element_type=jnp.float32
        )

    mixed = lax.fori_loop(0, steps, mix_block, jnp.zeros((count, heads, HEAD_DIM), jnp.float32))
    if fresh_key is not None:
        own_weight = jnp.exp(own - top)
        total = total + own_weight
        mixed = mixed + own_weight.astype(jnp.bfloat16).astype(jnp.float32)[
            :, :, None
        ] * fresh_value.reshape(count, heads, HEAD_DIM).astype(jnp.float32)
    return (mixed / total[:, :, None]).astype(jnp.bfloat16).reshape(count, width)


def decode_layer(
    tokens, self_keys, self_values, self_len, cross_keys, cross_values, cross_len, params
):
    (
        w_query,
        w_key,
        w_value,
        w_out,
        w_cross_query,
        w_cross_out,
        w_up,
        w_down,
        gain_self,
        gain_cross,
        gain_final,
    ) = params
    scale = HEAD_DIM ** (-0.5)
    query = (jnp.dot(tokens, w_query, preferred_element_type=jnp.float32) * scale).astype(
        jnp.bfloat16
    )
    fresh_keys = jnp.dot(tokens, w_key, preferred_element_type=jnp.float32).astype(jnp.bfloat16)
    fresh_values = jnp.dot(tokens, w_value, preferred_element_type=jnp.float32).astype(jnp.bfloat16)
    self_mixed = attend(query, self_keys, self_values, self_len, fresh_keys, fresh_values)
    self_total = lax.psum(jnp.dot(self_mixed, w_out, preferred_element_type=jnp.float32), "head")
    first = layer_norm(tokens.astype(jnp.float32) + self_total, gain_self).astype(jnp.bfloat16)
    cross_query = (
        jnp.dot(first, w_cross_query, preferred_element_type=jnp.float32) * scale
    ).astype(jnp.bfloat16)
    cross_mixed = attend(cross_query, cross_keys, cross_values, cross_len, None, None)
    cross_total = lax.psum(
        jnp.dot(cross_mixed, w_cross_out, preferred_element_type=jnp.float32), "head"
    )
    second = layer_norm(first.astype(jnp.float32) + cross_total, gain_cross).astype(jnp.bfloat16)
    hidden = jax.nn.gelu(
        jnp.dot(second, w_up, preferred_element_type=jnp.float32), approximate=False
    ).astype(jnp.bfloat16)
    ffn_total = lax.psum(jnp.dot(hidden, w_down, preferred_element_type=jnp.float32), "head")
    layer_out = layer_norm(second.astype(jnp.float32) + ffn_total, gain_final).astype(jnp.bfloat16)
    return (layer_out, fresh_keys, fresh_values)


def take_slot(array, chosen):
    return lax.dynamic_slice_in_dim(array, chosen, 1, 0)


def put_slot(array, row, chosen):
    return lax.dynamic_update_slice_in_dim(array, row, chosen, 0)


def on_device(
    tokens,
    self_keys,
    self_values,
    self_len,
    cross_keys,
    cross_values,
    cross_len,
    give_slot,
    w_query,
    w_key,
    w_value,
    w_out,
    w_cross_query,
    w_cross_out,
    w_up,
    w_down,
    gain_self,
    gain_cross,
    gain_final,
):
    params = (
        w_query,
        w_key,
        w_value,
        w_out,
        w_cross_query,
        w_cross_out,
        w_up,
        w_down,
        gain_self,
        gain_cross,
        gain_final,
    )
    chosen = give_slot[0]
    half_axis = lax.axis_size("req") // 2
    moving = passed_along(
        (
            take_slot(tokens, chosen),
            take_slot(self_keys, chosen),
            take_slot(self_values, chosen),
            take_slot(cross_keys, chosen),
            take_slot(cross_values, chosen),
        ),
        "req",
        half_axis,
    )
    arrived_len = passed_along(
        (take_slot(self_len, chosen), take_slot(cross_len, chosen)), "req", half_axis
    )
    decoded, new_keys, new_values = decode_layer(
        put_slot(tokens, moving[0], chosen),
        put_slot(self_keys, moving[1], chosen),
        put_slot(self_values, moving[2], chosen),
        put_slot(self_len, arrived_len[0], chosen),
        put_slot(cross_keys, moving[3], chosen),
        put_slot(cross_values, moving[4], chosen),
        put_slot(cross_len, arrived_len[1], chosen),
        params,
    )
    moved_keys = moving[1]
    moved_values = moving[2]
    return (decoded, new_keys, new_values, moved_keys, moved_values)


def solution(mesh):
    placed = (
        P("req", None),
        P("req", None, "head"),
        P("req", None, "head"),
        P("req"),
        P("req", None, "head"),
        P("req", None, "head"),
        P("req"),
        P("req"),
        P(None, "head"),
        P(None, "head"),
        P(None, "head"),
        P("head", None),
        P(None, "head"),
        P("head", None),
        P(None, "head"),
        P("head", None),
        P(),
        P(),
        P(),
    )
    return jax.shard_map(
        on_device,
        mesh=mesh,
        in_specs=placed,
        out_specs=(
            P("req", None),
            P("req", "head"),
            P("req", "head"),
            P("req", None, "head"),
            P("req", None, "head"),
        ),
        check_vma=False,
    )
```

profile of v0, /device:TPU:1, one launch (start us, length us, event | category | flops | bytes accessed | tf_op | source)
XLA Modules:
  0.0 135.8 jit_solution(12069132178219028557)
XLA Ops:
  0.6 0.7 copy.88
  1.4 0.7 copy.87
  2.8 0.6 dynamic_slice.22
  3.3 16.2 %collective-permute-start.1 = (s32[1]{0:T(128)}, s32[1]{0:T(128)}, u32[]{:S(2)}, u32[]{:S(2)}) collective-permute-start(s32[1]{0:T(128)} %dynamic_slice.22), channel_id=1, source_target_pairs={{256,0},{264,8},{272,16},{280,24},{288,32},{296,40},{304,48},{312,... | collective-permute-start | bytes 20 | tf_op jit(solution)/shard_map/ppermute | solution.py:12
  19.6 1.9 %collective-permute-start = (bf16[1,1024]{1,0:T(2,128)(2,1)S(1)}, bf16[1,1024]{1,0:T(2,128)(2,1)S(1)}, u32[]{:S(2)}, u32[]{:S(2)}) collective-permute-start(bf16[1,1024]{1,0:T(2,128)(2,1)S(1)} %constant_dynamic-slice_fusion.4), channel_id=1, source_target_pairs={{256,0},{264,8},{272,16},{280,24},{288,32},{296,40},{304,48},{312,... | collective-permute-start | bytes 6152 | tf_op jit(solution)/shard_map/ppermute | solution.py:12
  21.6 1.1 copy.25
  22.7 0.7 constant_dynamic-slice_fusion.3
  23.3 12.1 %collective-permute-start.2 = (bf16[1,512,128]{1,2,0:T(8,128)(2,1)}, bf16[1,512,128]{1,2,0:T(8,128)(2,1)S(1)}, u32[]{:S(2)}, u32[]{:S(2)}) collective-permute-start(bf16[1,512,128]{1,2,0:T(8,128)(2,1)} %constant_dynamic-slice_fusion.3), channel_id=1, source_target_pairs={{256,0},{264,8},{272,16},{280,24},{288,32},{296,40},{304,48},{312,... | collective-permute-start | bytes 393224 | tf_op jit(solution)/shard_map/ppermute | solution.py:12
  35.6 2.1 %collective-permute-start.3 = (bf16[1,512,128]{1,2,0:T(8,128)(2,1)S(1)}, bf16[1,512,128]{1,2,0:T(8,128)(2,1)S(1)}, u32[]{:S(2)}, u32[]{:S(2)}) collective-permute-start(bf16[1,512,128]{1,2,0:T(8,128)(2,1)S(1)} %constant_dynamic-slice_fusion.2), channel_id=1, source_target_pairs={{256,0},{264,8},{272,16},{280,24},{288,32},{296,40},{304,48},{312,... | collective-permute-start | bytes 393224 | tf_op jit(solution)/shard_map/ppermute | solution.py:12
  37.8 0.7 constant_dynamic-slice_fusion.1
  38.5 12.1 %collective-permute-start.5 = (bf16[1,512,128]{1,2,0:T(8,128)(2,1)}, bf16[1,512,128]{1,2,0:T(8,128)(2,1)S(1)}, u32[]{:S(2)}, u32[]{:S(2)}) collective-permute-start(bf16[1,512,128]{1,2,0:T(8,128)(2,1)} %constant_dynamic-slice_fusion.1), channel_id=1, source_target_pairs={{256,0},{264,8},{272,16},{280,24},{288,32},{296,40},{304,48},{312,... | collective-permute-start | bytes 393224 | tf_op jit(solution)/shard_map/ppermute | solution.py:12
  50.6 0.6 dynamic_slice.25
  51.4 2.1 %collective-permute-start.4 = (s32[1]{0:T(128)}, s32[1]{0:T(128)}, u32[]{:S(2)}, u32[]{:S(2)}) collective-permute-start(s32[1]{0:T(128)} %dynamic_slice.25), channel_id=1, source_target_pairs={{256,0},{264,8},{272,16},{280,24},{288,32},{296,40},{304,48},{312,... | collective-permute-start | bytes 20 | tf_op jit(solution)/shard_map/ppermute | solution.py:12
  53.4 0.8 dynamic_update_slice.22
  54.2 0.6 reduce_max.36
  55.5 16.9 %collective-permute-done.4 = s32[1]{0:T(128)} collective-permute-done((s32[1]{0:T(128)}, s32[1]{0:T(128)}, u32[]{:S(2)}, u32[]{:S(2)}) %collective-permute-start.4) | collective-permute-done | bytes 36 | tf_op jit(solution)/shard_map/ppermute | solution.py:12
  72.4 4.9 %collective-permute-start.6 = (bf16[1,512,128]{1,2,0:T(8,128)(2,1)S(1)}, bf16[1,512,128]{1,2,0:T(8,128)(2,1)S(1)}, u32[]{:S(2)}, u32[]{:S(2)}) collective-permute-start(bf16[1,512,128]{1,2,0:T(8,128)(2,1)S(1)} %constant_dynamic-slice_fusion), channel_id=1, source_target_pairs={{256,0},{264,8},{272,16},{280,24},{288,32},{296,40},{304,48},{312,... | collective-permute-start | bytes 393224 | tf_op jit(solution)/shard_map/ppermute | solution.py:12
  77.3 0.7 dynamic_update_slice.25
  78.1 0.6 reduce_max.38
  79.5 0.2 fusion.7
  79.7 0.2 convolution_convert_fusion.1
  79.8 0.6 copy-done.7
  80.4 0.1 convolution_convert_fusion
  80.8 0.2 copy-done.15
  81.5 0.6 broadcast.133.clone
  82.1 0.7 while.52
  82.1 0.6 broadcast_select_fusion.4
  82.8 0.9 reduce_max.37
  83.6 0.2 fusion.13
  83.8 0.2 fusion.11
  84.2 0.6 copy-done.8
  84.9 16.8 %psum.21 = f32[2,1024]{1,0:T(2,128)S(1)} all-reduce(f32[2,1024]{1,0:T(2,128)S(1)} %fusion.92), channel_id=1, replica_groups=mesh['req'=64,'head'=8] {'head'}, use_global_device_ids=true, to_apply=%region_8.9 | all-reduce | flops 2048 | bytes 16384 | tf_op jit(solution)/shard_map/psum | solution.py:93
  101.9 0.2 multiply_reduce_fusion.2
  102.2 0.1 fusion.8
  102.6 0.6 broadcast.133
  103.2 0.7 while.53
  103.3 0.6 broadcast_select_fusion.5
  103.9 0.9 fusion.6
  104.9 0.2 fusion.9
  105.2 0.6 copy-done.10
  106.0 13.7 %psum.22 = f32[2,1024]{1,0:T(2,128)S(1)} all-reduce(f32[2,1024]{1,0:T(2,128)S(1)} %fusion.94), channel_id=1, replica_groups=mesh['req'=64,'head'=8] {'head'}, use_global_device_ids=true, to_apply=%region_18.19 | all-reduce | flops 2048 | bytes 16384 | tf_op jit(solution)/shard_map/psum | solution.py:99
  119.8 0.2 multiply_reduce_fusion.1
  120.1 0.5 fusion.21
  120.6 12.6 %psum.23 = f32[2,1024]{1,0:T(2,128)S(1)} all-reduce(f32[2,1024]{1,0:T(2,128)S(1)} %fusion.21), channel_id=1, replica_groups=mesh['req'=64,'head'=8] {'head'}, use_global_device_ids=true, to_apply=%region_21.22 | all-reduce | flops 2048 | bytes 16384 | tf_op jit(solution)/shard_map/psum | solution.py:106
  133.4 0.2 multiply_reduce_fusion
  133.6 0.7 multiply_convert_fusion
  134.3 0.8 copy.32
  135.0 0.8 copy.33
  (90 shorter events, 3.1 us)
Async XLA Ops:
  0.6 119.4 %copy-start = (bf16[512,1024]{1,0:T(8,128)(2,1)S(1)}, bf16[512,1024]{1,0:T(8,128)(2,1)}, u32[]{:S(2)}) copy-start(bf16[512,1024]{1,0:T(8,128)(2,1)} %param.42) | copy-start | bytes 3145732
  1.4 0.7 copy-start.17
  3.3 48.0 %collective-permute-start.1 = (s32[1]{0:T(128)}, s32[1]{0:T(128)}, u32[]{:S(2)}, u32[]{:S(2)}) collective-permute-start(s32[1]{0:T(128)} %dynamic_slice.22), channel_id=1, source_target_pairs={{256,0},{264,8},{272,16},{280,24},{288,32},{296,40},{304,48},{312,... | collective-permute-start | bytes 20 | tf_op jit(solution)/shard_map/ppermute | solution.py:12
  19.6 59.8 %collective-permute-start = (bf16[1,1024]{1,0:T(2,128)(2,1)S(1)}, bf16[1,1024]{1,0:T(2,128)(2,1)S(1)}, u32[]{:S(2)}, u32[]{:S(2)}) collective-permute-start(bf16[1,1024]{1,0:T(2,128)(2,1)S(1)} %constant_dynamic-slice_fusion.4), channel_id=1, source_target_pairs={{256,0},{264,8},{272,16},{280,24},{288,32},{296,40},{304,48},{312,... | collective-permute-start | bytes 6152 | tf_op jit(solution)/shard_map/ppermute | solution.py:12
  22.6 12.8 %copy-start.2 = (bf16[2,512,128]{2,1,0:T(8,128)(2,1)S(1)}, bf16[2,512,128]{2,1,0:T(8,128)(2,1)}, u32[]{:S(2)}) copy-start(bf16[2,512,128]{2,1,0:T(8,128)(2,1)} %param.29) | copy-start | bytes 786436
  23.3 58.0 %collective-permute-start.2 = (bf16[1,512,128]{1,2,0:T(8,128)(2,1)}, bf16[1,512,128]{1,2,0:T(8,128)(2,1)S(1)}, u32[]{:S(2)}, u32[]{:S(2)}) collective-permute-start(bf16[1,512,128]{1,2,0:T(8,128)(2,1)} %constant_dynamic-slice_fusion.3), channel_id=1, source_target_pairs={{256,0},{264,8},{272,16},{280,24},{288,32},{296,40},{304,48},{312,... | collective-permute-start | bytes 393224 | tf_op jit(solution)/shard_map/ppermute | solution.py:12
  35.6 2.1 %copy-start.3 = (bf16[2,512,128]{2,1,0:T(8,128)(2,1)S(1)}, bf16[2,512,128]{2,1,0:T(8,128)(2,1)}, u32[]{:S(2)}) copy-start(bf16[2,512,128]{2,1,0:T(8,128)(2,1)} %param.31) | copy-start | bytes 786436
  35.6 48.2 %collective-permute-start.3 = (bf16[1,512,128]{1,2,0:T(8,128)(2,1)S(1)}, bf16[1,512,128]{1,2,0:T(8,128)(2,1)S(1)}, u32[]{:S(2)}, u32[]{:S(2)}) collective-permute-start(bf16[1,512,128]{1,2,0:T(8,128)(2,1)S(1)} %constant_dynamic-slice_fusion.2), channel_id=1, source_target_pairs={{256,0},{264,8},{272,16},{280,24},{288,32},{296,40},{304,48},{312,... | collective-permute-start | bytes 393224 | tf_op jit(solution)/shard_map/ppermute | solution.py:12
  37.8 13.3 %copy-start.4 = (bf16[2,512,128]{2,1,0:T(8,128)(2,1)S(1)}, bf16[2,512,128]{2,1,0:T(8,128)(2,1)}, u32[]{:S(2)}) copy-start(bf16[2,512,128]{2,1,0:T(8,128)(2,1)} %param.32) | copy-start | bytes 786436
  38.5 63.9 %collective-permute-start.5 = (bf16[1,512,128]{1,2,0:T(8,128)(2,1)}, bf16[1,512,128]{1,2,0:T(8,128)(2,1)S(1)}, u32[]{:S(2)}, u32[]{:S(2)}) collective-permute-start(bf16[1,512,128]{1,2,0:T(8,128)(2,1)} %constant_dynamic-slice_fusion.1), channel_id=1, source_target_pairs={{256,0},{264,8},{272,16},{280,24},{288,32},{296,40},{304,48},{312,... | collective-permute-start | bytes 393224 | tf_op jit(solution)/shard_map/ppermute | solution.py:12
  51.3 28.2 %copy-start.5 = (bf16[1024,128]{1,0:T(8,128)(2,1)S(1)}, bf16[1024,128]{1,0:T(8,128)(2,1)}, u32[]{:S(2)}) copy-start(bf16[1024,128]{1,0:T(8,128)(2,1)} %param.35) | copy-start | bytes 786436
  51.3 28.3 %copy-start.6 = (bf16[1024,128]{1,0:T(8,128)(2,1)S(1)}, bf16[1024,128]{1,0:T(8,128)(2,1)}, u32[]{:S(2)}) copy-start(bf16[1024,128]{1,0:T(8,128)(2,1)} %param.36) | copy-start | bytes 786436
  51.4 21.0 %collective-permute-start.4 = (s32[1]{0:T(128)}, s32[1]{0:T(128)}, u32[]{:S(2)}, u32[]{:S(2)}) collective-permute-start(s32[1]{0:T(128)} %dynamic_slice.25), channel_id=1, source_target_pairs={{256,0},{264,8},{272,16},{280,24},{288,32},{296,40},{304,48},{312,... | collective-permute-start | bytes 20 | tf_op jit(solution)/shard_map/ppermute | solution.py:12
  72.4 32.4 %collective-permute-start.6 = (bf16[1,512,128]{1,2,0:T(8,128)(2,1)S(1)}, bf16[1,512,128]{1,2,0:T(8,128)(2,1)S(1)}, u32[]{:S(2)}, u32[]{:S(2)}) collective-permute-start(bf16[1,512,128]{1,2,0:T(8,128)(2,1)S(1)} %constant_dynamic-slice_fusion), channel_id=1, source_target_pairs={{256,0},{264,8},{272,16},{280,24},{288,32},{296,40},{304,48},{312,... | collective-permute-start | bytes 393224 | tf_op jit(solution)/shard_map/ppermute | solution.py:12
  79.5 1.0 copy-start.7
  80.4 0.5 copy-start.15
  80.6 0.5 copy-start.16
  82.8 0.9 copy-start.11
  83.8 1.0 copy-start.8
  84.0 18.1 %copy-start.9 = (bf16[1024,128]{1,0:T(8,128)(2,1)S(1)}, bf16[1024,128]{1,0:T(8,128)(2,1)}, u32[]{:S(2)}) copy-start(bf16[1024,128]{1,0:T(8,128)(2,1)} %param.39) | copy-start | bytes 786436
  84.8 17.3 %copy-start.12 = (f32[1024]{0:T(1024)S(1)}, f32[1024]{0:T(1024)}, u32[]{:S(2)}) copy-start(f32[1024]{0:T(1024)} %param.43) | copy-start | bytes 12292
  102.1 17.9 %copy-start.1 = (bf16[1024,512]{1,0:T(8,128)(2,1)S(1)}, bf16[1024,512]{1,0:T(8,128)(2,1)}, u32[]{:S(2)}) copy-start(bf16[1024,512]{1,0:T(8,128)(2,1)} %param.41) | copy-start | bytes 3145732
  104.8 1.0 copy-start.10
  105.8 14.2 %copy-start.13 = (f32[1024]{0:T(1024)S(1)}, f32[1024]{0:T(1024)}, u32[]{:S(2)}) copy-start(f32[1024]{0:T(1024)} %param.44) | copy-start | bytes 12292
  120.1 13.5 %copy-start.14 = (f32[1024]{0:T(1024)S(1)}, f32[1024]{0:T(1024)}, u32[]{:S(2)}) copy-start(f32[1024]{0:T(1024)} %param.45) | copy-start | bytes 12292
where the time goes:
time: 136 us
  starting transfers between devices  51.3 us (38%)
  blocking collectives  43.1 us (32%)
  waiting for transfers between devices  16.9 us (12%)
  local copies, waits for them, and re-layouts  12.7 us (9%)
  other arithmetic  6.73 us (5%)
  between operations  3.02 us (2%)
  matrix products  2 us (1%)
    ppermute x7, starting transfers between devices, passed_along(): return lax.ppermute(block, axis, route)  51.3 us
    ppermute x7, waiting for transfers between devices, passed_along(): return lax.ppermute(block, axis, route)  16.9 us
    psum x1, blocking collectives, decode_layer(): lax.psum(jnp.dot(self_mixed, w_out, preferred_element_type=jnp.float32),...  16.8 us
    psum x1, blocking collectives, decode_layer(): lax.psum(jnp.dot(cross_mixed, w_cross_out, preferred_element_type=jnp.flo...  13.7 us
    psum x1, blocking collectives, decode_layer(): lax.psum(jnp.dot(hidden, w_down, preferred_element_type=jnp.float32), 'he...  12.6 us
    unnamed x45, local copies, waits for them, and re-layouts  6.63 us
  transfers between devices with their start and end apart: 7, of which 1 were waited for; matrix products, arithmetic and copies ran while one was open for 10% of the time, Pallas kernels for 0%

commit v1 on v0

--- a/solution.py
+++ b/solution.py
@@ -103,7 +103,9 @@
     hidden = jax.nn.gelu(
         jnp.dot(second, w_up, preferred_element_type=jnp.float32), approximate=False
     ).astype(jnp.bfloat16)
-    ffn_total = lax.psum(jnp.dot(hidden, w_down, preferred_element_type=jnp.float32), "head")
+    ffn_total = jnp.sum(
+        lax.all_gather(jnp.dot(hidden, w_down, preferred_element_type=jnp.float32), "head"), axis=0
+    )
     layer_out = layer_norm(second.astype(jnp.float32) + ffn_total, gain_final).astype(jnp.bfloat16)
     return (layer_out, fresh_keys, fresh_values)
 

time: 136 us -> 137 us (level)
    all_gather x0 -> x1, blocking collectives: none -> 13.4 us  [decode_layer(): lax.all_gather(jnp.dot(hidden, w_down, preferred_element_type=jnp.float32...]
    psum x1 -> x0, blocking collectives: 12.6 us -> none  [decode_layer(): lax.psum(jnp.dot(hidden, w_down, preferred_element_type=jnp.float32), 'he...]
where the time goes in v1:
time: 137 us
  starting transfers between devices  51.3 us (37%)
  blocking collectives  43.9 us (32%)
  waiting for transfers between devices  16.9 us (12%)
  local copies, waits for them, and re-layouts  12.7 us (9%)
  other arithmetic  6.76 us (5%)
  between operations  3.01 us (2%)
  matrix products  2 us (1%)
    ppermute x7, starting transfers between devices, passed_along(): return lax.ppermute(block, axis, route)  51.3 us
    ppermute x7, waiting for transfers between devices, passed_along(): return lax.ppermute(block, axis, route)  16.9 us
    psum x1, blocking collectives, decode_layer(): lax.psum(jnp.dot(self_mixed, w_out, preferred_element_type=jnp.float32),...  16.8 us
    psum x1, blocking collectives, decode_layer(): lax.psum(jnp.dot(cross_mixed, w_cross_out, preferred_element_type=jnp.flo...  13.7 us
    all_gather x1, blocking collectives, decode_layer(): lax.all_gather(jnp.dot(hidden, w_down, preferred_element_type=jnp.float32...  13.4 us
    unnamed x45, local copies, waits for them, and re-layouts  6.63 us
  transfers between devices with their start and end apart: 7, of which 1 were waited for; matrix products, arithmetic and copies ran while one was open for 10% of the time, Pallas kernels for 0%

profile of v1, /device:TPU:1, one launch (start us, length us, event | category | flops | bytes accessed | tf_op | source)
XLA Modules:
  0.0 136.6 jit_solution(9257621517263688226)
XLA Ops:
  0.6 0.7 copy.99
  1.4 0.7 copy.98
  2.8 0.6 dynamic_slice.22
  3.3 16.2 %collective-permute-start.1 = (s32[1]{0:T(128)}, s32[1]{0:T(128)}, u32[]{:S(2)}, u32[]{:S(2)}) collective-permute-start(s32[1]{0:T(128)} %dynamic_slice.22), channel_id=1, source_target_pairs={{256,0},{264,8},{272,16},{280,24},{288,32},{296,40},{304,48},{312,... | collective-permute-start | bytes 20 | tf_op jit(solution)/shard_map/ppermute | solution.py:12
  19.6 1.9 %collective-permute-start = (bf16[1,1024]{1,0:T(2,128)(2,1)S(1)}, bf16[1,1024]{1,0:T(2,128)(2,1)S(1)}, u32[]{:S(2)}, u32[]{:S(2)}) collective-permute-start(bf16[1,1024]{1,0:T(2,128)(2,1)S(1)} %constant_dynamic-slice_fusion.4), channel_id=1, source_target_pairs={{256,0},{264,8},{272,16},{280,24},{288,32},{296,40},{304,48},{312,... | collective-permute-start | bytes 6152 | tf_op jit(solution)/shard_map/ppermute | solution.py:12
  21.6 1.1 copy.35
  22.7 0.7 constant_dynamic-slice_fusion.3
  23.3 12.1 %collective-permute-start.2 = (bf16[1,512,128]{1,2,0:T(8,128)(2,1)}, bf16[1,512,128]{1,2,0:T(8,128)(2,1)S(1)}, u32[]{:S(2)}, u32[]{:S(2)}) collective-permute-start(bf16[1,512,128]{1,2,0:T(8,128)(2,1)} %constant_dynamic-slice_fusion.3), channel_id=1, source_target_pairs={{256,0},{264,8},{272,16},{280,24},{288,32},{296,40},{304,48},{312,... | collective-permute-start | bytes 393224 | tf_op jit(solution)/shard_map/ppermute | solution.py:12
  35.6 2.1 %collective-permute-start.3 = (bf16[1,512,128]{1,2,0:T(8,128)(2,1)S(1)}, bf16[1,512,128]{1,2,0:T(8,128)(2,1)S(1)}, u32[]{:S(2)}, u32[]{:S(2)}) collective-permute-start(bf16[1,512,128]{1,2,0:T(8,128)(2,1)S(1)} %constant_dynamic-slice_fusion.2), channel_id=1, source_target_pairs={{256,0},{264,8},{272,16},{280,24},{288,32},{296,40},{304,48},{312,... | collective-permute-start | bytes 393224 | tf_op jit(solution)/shard_map/ppermute | solution.py:12
  37.8 0.7 constant_dynamic-slice_fusion.1
  38.5 12.1 %collective-permute-start.5 = (bf16[1,512,128]{1,2,0:T(8,128)(2,1)}, bf16[1,512,128]{1,2,0:T(8,128)(2,1)S(1)}, u32[]{:S(2)}, u32[]{:S(2)}) collective-permute-start(bf16[1,512,128]{1,2,0:T(8,128)(2,1)} %constant_dynamic-slice_fusion.1), channel_id=1, source_target_pairs={{256,0},{264,8},{272,16},{280,24},{288,32},{296,40},{304,48},{312,... | collective-permute-start | bytes 393224 | tf_op jit(solution)/shard_map/ppermute | solution.py:12
  50.6 0.6 dynamic_slice.25
  51.4 2.1 %collective-permute-start.4 = (s32[1]{0:T(128)}, s32[1]{0:T(128)}, u32[]{:S(2)}, u32[]{:S(2)}) collective-permute-start(s32[1]{0:T(128)} %dynamic_slice.25), channel_id=1, source_target_pairs={{256,0},{264,8},{272,16},{280,24},{288,32},{296,40},{304,48},{312,... | collective-permute-start | bytes 20 | tf_op jit(solution)/shard_map/ppermute | solution.py:12
  53.4 0.8 dynamic_update_slice.22
  54.2 0.6 reduce_max.36
  55.5 16.9 %collective-permute-done.4 = s32[1]{0:T(128)} collective-permute-done((s32[1]{0:T(128)}, s32[1]{0:T(128)}, u32[]{:S(2)}, u32[]{:S(2)}) %collective-permute-start.4) | collective-permute-done | bytes 36 | tf_op jit(solution)/shard_map/ppermute | solution.py:12
  72.4 4.9 %collective-permute-start.6 = (bf16[1,512,128]{1,2,0:T(8,128)(2,1)S(1)}, bf16[1,512,128]{1,2,0:T(8,128)(2,1)S(1)}, u32[]{:S(2)}, u32[]{:S(2)}) collective-permute-start(bf16[1,512,128]{1,2,0:T(8,128)(2,1)S(1)} %constant_dynamic-slice_fusion), channel_id=1, source_target_pairs={{256,0},{264,8},{272,16},{280,24},{288,32},{296,40},{304,48},{312,... | collective-permute-start | bytes 393224 | tf_op jit(solution)/shard_map/ppermute | solution.py:12
  77.3 0.7 dynamic_update_slice.25
  78.1 0.6 reduce_max.38
  79.5 0.2 fusion.7
  79.7 0.2 convolution_convert_fusion.1
  79.8 0.6 copy-done.7
  80.4 0.1 convolution_convert_fusion
  80.8 0.2 copy-done.15
  81.5 0.6 broadcast.133.clone
  82.1 0.7 while.52
  82.1 0.6 broadcast_select_fusion.4
  82.8 0.9 reduce_max.37
  83.6 0.2 fusion.13
  83.8 0.2 fusion.11
  84.2 0.6 copy-done.8
  84.9 16.8 %psum.14 = f32[2,1024]{1,0:T(2,128)S(1)} all-reduce(f32[2,1024]{1,0:T(2,128)S(1)} %fusion.91), channel_id=1, replica_groups=mesh['req'=64,'head'=8] {'head'}, use_global_device_ids=true, to_apply=%region_8.9 | all-reduce | flops 2048 | bytes 16384 | tf_op jit(solution)/shard_map/psum | solution.py:93
  101.9 0.2 multiply_reduce_fusion.2
  102.2 0.1 fusion.8
  102.6 0.6 broadcast.133
  103.2 0.7 while.53
  103.3 0.6 broadcast_select_fusion.5
  103.9 0.9 fusion.6
  104.9 0.2 fusion.9
  105.2 0.6 copy-done.10
  106.0 13.7 %psum.15 = f32[2,1024]{1,0:T(2,128)S(1)} all-reduce(f32[2,1024]{1,0:T(2,128)S(1)} %fusion.93), channel_id=1, replica_groups=mesh['req'=64,'head'=8] {'head'}, use_global_device_ids=true, to_apply=%region_18.19 | all-reduce | flops 2048 | bytes 16384 | tf_op jit(solution)/shard_map/psum | solution.py:99
  119.8 0.2 multiply_reduce_fusion.1
  120.1 0.5 convolution_bitcast_fusion
  120.6 13.4 %all-gather.1 = f32[8,2,1024]{2,1,0:T(2,128)S(1)} all-gather(f32[1,2,1024]{2,1,0:T(2,128)S(1)} %convolution_bitcast_fusion), channel_id=2, replica_groups=mesh['req'=64,'head'=8] {'head'}, dimensions={0}, use_global_device_ids=true | all-gather | bytes 73728 | tf_op jit(solution)/shard_map/all_gather | solution.py:107
  134.2 0.2 multiply_reduce_fusion
  134.4 0.7 multiply_convert_fusion
  135.0 0.8 copy.42
  135.8 0.8 copy.43
  (91 shorter events, 3.1 us)
Async XLA Ops:
  0.6 119.4 %copy-start = (bf16[512,1024]{1,0:T(8,128)(2,1)S(1)}, bf16[512,1024]{1,0:T(8,128)(2,1)}, u32[]{:S(2)}) copy-start(bf16[512,1024]{1,0:T(8,128)(2,1)} %param.42) | copy-start | bytes 3145732
  1.4 0.7 copy-start.17
  3.3 48.0 %collective-permute-start.1 = (s32[1]{0:T(128)}, s32[1]{0:T(128)}, u32[]{:S(2)}, u32[]{:S(2)}) collective-permute-start(s32[1]{0:T(128)} %dynamic_slice.22), channel_id=1, source_target_pairs={{256,0},{264,8},{272,16},{280,24},{288,32},{296,40},{304,48},{312,... | collective-permute-start | bytes 20 | tf_op jit(solution)/shard_map/ppermute | solution.py:12
  19.6 59.8 %collective-permute-start = (bf16[1,1024]{1,0:T(2,128)(2,1)S(1)}, bf16[1,1024]{1,0:T(2,128)(2,1)S(1)}, u32[]{:S(2)}, u32[]{:S(2)}) collective-permute-start(bf16[1,1024]{1,0:T(2,128)(2,1)S(1)} %constant_dynamic-slice_fusion.4), channel_id=1, source_target_pairs={{256,0},{264,8},{272,16},{280,24},{288,32},{296,40},{304,48},{312,... | collective-permute-start | bytes 6152 | tf_op jit(solution)/shard_map/ppermute | solution.py:12
  22.6 12.8 %copy-start.2 = (bf16[2,512,128]{2,1,0:T(8,128)(2,1)S(1)}, bf16[2,512,128]{2,1,0:T(8,128)(2,1)}, u32[]{:S(2)}) copy-start(bf16[2,512,128]{2,1,0:T(8,128)(2,1)} %param.29) | copy-start | bytes 786436
  23.3 58.0 %collective-permute-start.2 = (bf16[1,512,128]{1,2,0:T(8,128)(2,1)}, bf16[1,512,128]{1,2,0:T(8,128)(2,1)S(1)}, u32[]{:S(2)}, u32[]{:S(2)}) collective-permute-start(bf16[1,512,128]{1,2,0:T(8,128)(2,1)} %constant_dynamic-slice_fusion.3), channel_id=1, source_target_pairs={{256,0},{264,8},{272,16},{280,24},{288,32},{296,40},{304,48},{312,... | collective-permute-start | bytes 393224 | tf_op jit(solution)/shard_map/ppermute | solution.py:12
  35.6 2.1 %copy-start.3 = (bf16[2,512,128]{2,1,0:T(8,128)(2,1)S(1)}, bf16[2,512,128]{2,1,0:T(8,128)(2,1)}, u32[]{:S(2)}) copy-start(bf16[2,512,128]{2,1,0:T(8,128)(2,1)} %param.31) | copy-start | bytes 786436
  35.6 48.2 %collective-permute-start.3 = (bf16[1,512,128]{1,2,0:T(8,128)(2,1)S(1)}, bf16[1,512,128]{1,2,0:T(8,128)(2,1)S(1)}, u32[]{:S(2)}, u32[]{:S(2)}) collective-permute-start(bf16[1,512,128]{1,2,0:T(8,128)(2,1)S(1)} %constant_dynamic-slice_fusion.2), channel_id=1, source_target_pairs={{256,0},{264,8},{272,16},{280,24},{288,32},{296,40},{304,48},{312,... | collective-permute-start | bytes 393224 | tf_op jit(solution)/shard_map/ppermute | solution.py:12
  37.8 13.3 %copy-start.4 = (bf16[2,512,128]{2,1,0:T(8,128)(2,1)S(1)}, bf16[2,512,128]{2,1,0:T(8,128)(2,1)}, u32[]{:S(2)}) copy-start(bf16[2,512,128]{2,1,0:T(8,128)(2,1)} %param.32) | copy-start | bytes 786436
  38.5 63.9 %collective-permute-start.5 = (bf16[1,512,128]{1,2,0:T(8,128)(2,1)}, bf16[1,512,128]{1,2,0:T(8,128)(2,1)S(1)}, u32[]{:S(2)}, u32[]{:S(2)}) collective-permute-start(bf16[1,512,128]{1,2,0:T(8,128)(2,1)} %constant_dynamic-slice_fusion.1), channel_id=1, source_target_pairs={{256,0},{264,8},{272,16},{280,24},{288,32},{296,40},{304,48},{312,... | collective-permute-start | bytes 393224 | tf_op jit(solution)/shard_map/ppermute | solution.py:12
  51.3 28.2 %copy-start.5 = (bf16[1024,128]{1,0:T(8,128)(2,1)S(1)}, bf16[1024,128]{1,0:T(8,128)(2,1)}, u32[]{:S(2)}) copy-start(bf16[1024,128]{1,0:T(8,128)(2,1)} %param.35) | copy-start | bytes 786436
  51.3 28.3 %copy-start.6 = (bf16[1024,128]{1,0:T(8,128)(2,1)S(1)}, bf16[1024,128]{1,0:T(8,128)(2,1)}, u32[]{:S(2)}) copy-start(bf16[1024,128]{1,0:T(8,128)(2,1)} %param.36) | copy-start | bytes 786436
  51.4 21.0 %collective-permute-start.4 = (s32[1]{0:T(128)}, s32[1]{0:T(128)}, u32[]{:S(2)}, u32[]{:S(2)}) collective-permute-start(s32[1]{0:T(128)} %dynamic_slice.25), channel_id=1, source_target_pairs={{256,0},{264,8},{272,16},{280,24},{288,32},{296,40},{304,48},{312,... | collective-permute-start | bytes 20 | tf_op jit(solution)/shard_map/ppermute | solution.py:12
  72.4 32.4 %collective-permute-start.6 = (bf16[1,512,128]{1,2,0:T(8,128)(2,1)S(1)}, bf16[1,512,128]{1,2,0:T(8,128)(2,1)S(1)}, u32[]{:S(2)}, u32[]{:S(2)}) collective-permute-start(bf16[1,512,128]{1,2,0:T(8,128)(2,1)S(1)} %constant_dynamic-slice_fusion), channel_id=1, source_target_pairs={{256,0},{264,8},{272,16},{280,24},{288,32},{296,40},{304,48},{312,... | collective-permute-start | bytes 393224 | tf_op jit(solution)/shard_map/ppermute | solution.py:12
  79.5 1.0 copy-start.7
  80.4 0.5 copy-start.15
  80.6 0.5 copy-start.16
  82.8 0.9 copy-start.11
  83.8 1.0 copy-start.8
  84.0 18.1 %copy-start.9 = (bf16[1024,128]{1,0:T(8,128)(2,1)S(1)}, bf16[1024,128]{1,0:T(8,128)(2,1)}, u32[]{:S(2)}) copy-start(bf16[1024,128]{1,0:T(8,128)(2,1)} %param.39) | copy-start | bytes 786436
  84.8 17.3 %copy-start.12 = (f32[1024]{0:T(1024)S(1)}, f32[1024]{0:T(1024)}, u32[]{:S(2)}) copy-start(f32[1024]{0:T(1024)} %param.43) | copy-start | bytes 12292
  102.1 17.9 %copy-start.1 = (bf16[1024,512]{1,0:T(8,128)(2,1)S(1)}, bf16[1024,512]{1,0:T(8,128)(2,1)}, u32[]{:S(2)}) copy-start(bf16[1024,512]{1,0:T(8,128)(2,1)} %param.41) | copy-start | bytes 3145732
  104.8 1.0 copy-start.10
  105.8 14.2 %copy-start.13 = (f32[1024]{0:T(1024)S(1)}, f32[1024]{0:T(1024)}, u32[]{:S(2)}) copy-start(f32[1024]{0:T(1024)} %param.44) | copy-start | bytes 12292
  120.6 13.8 %copy-start.14 = (f32[1024]{0:T(1024)S(1)}, f32[1024]{0:T(1024)}, u32[]{:S(2)}) copy-start(f32[1024]{0:T(1024)} %param.45) | copy-start | bytes 12292
